TPU v7x, 128 devices: a whole 4x4x4 slice. The times are simulated.
128 devices in a mesh: row: 8 (over y, core), col: 16 (over x, z).
Axes of the slice: x: 4, y: 4, z: 4, core: 2. Of those that a mesh axis runs over, the one named last changes fastest.
Arguments:
- occ_coeffs: bfloat16 [49152, 20480], P('row', 'col'), may hold values from -0.21875 to 0.21875
- colloc: bfloat16 [1024, 1024, 512], P(('row', 'col')), may hold values from -6 to 6
- grid_points: float32 [1024, 3, 512], P(('row', 'col')), may hold values from -4 to 4
- grid_weights: float32 [1024, 512], P(('row', 'col')), may hold values from 0.01 to 0.1
- charge_sites: float32 [3, 512], replicated, may hold values from -4 to 4
- charge_proj: bfloat16 [512, 128], replicated, may hold values from -0.5 to 0.5
- shell_lists: int32 [1024, 16], P(('row', 'col')), may hold values from 0 to 767, as said below
- point_counts: int32 [1024], P(('row', 'col')), may hold values from 1 to 512, as said below
Outputs:
- exchange_slab: float32 [49152, 128], P(('row', 'col'))
Inputs may be any that keep to these rules, and one draw needn't show every extreme that they name: `shell_lists`: batches b * 8 to b * 8 + 7 belong to the b-th device in row+col order, and the blocks named by one device's batches are all different. Owner device o holds blocks o * 6 to o * 6 + 5; one device's batches name at most 2 blocks of one owner, and in every draw one owner gets exactly 2 from every device. `point_counts`: points of a batch beyond its count are not part of it.
All inputs are finite; a program needn't handle non-finite values.
Results may differ from a plain program's by a relative error of at most 0.0045.
Values may be sent and summed in bfloat16 or wider, within the bound.
No kernel may reach another device: no remote copies, remote signals or barrier semaphores. Data moves between devices by JAX's collectives and lax.ppermute only.
A program may use at most 128 MiB of HBM per device.

v0:
```python
import jax
import jax.numpy as jnp
from jax import lax
from jax.sharding import PartitionSpec as P

SH = 64
NSIG = 16
smear_sq = 0.25


def broadcast_from_first(value, axis):
    size = lax.axis_size(axis)
    index = lax.axis_index(axis)
    have = 1
    while have < size:
        pairs = [(src, src + have) for src in range(have) if src + have < size]
        moved = lax.ppermute(value, axis, pairs)
        value = jnp.where(index >= have, moved, value)
        have *= 2
    return value


def potential(points, charge_sites):
    dist_sq = (points[:, 0][:, None, :] - charge_sites[0][None, :, None]) ** 2
    dist_sq = dist_sq + (points[:, 1][:, None, :] - charge_sites[1][None, :, None]) ** 2
    dist_sq = dist_sq + (points[:, 2][:, None, :] - charge_sites[2][None, :, None]) ** 2
    return lax.rsqrt(dist_sq + smear_sq)


def batch_terms(
    dens_rows, colloc, grid_points, grid_weights, charge_sites, charge_proj, point_counts
):
    total_points = colloc.shape[2]
    field = jnp.einsum(
        "bfs,bfp->bsp", dens_rows, colloc, preferred_element_type=jnp.float32
    ).astype(jnp.bfloat16)
    projected = jnp.einsum("ks,bsp->bkp", charge_proj, field, preferred_element_type=jnp.float32)
    live = (jnp.arange(total_points)[None, :] < point_counts[:, None]).astype(jnp.float32)
    charges = (
        projected * potential(grid_points, charge_sites) * (grid_weights * live)[:, None, :]
    ).astype(jnp.bfloat16)
    spread_back = jnp.einsum(
        "ks,bkp->bsp", charge_proj, charges, preferred_element_type=jnp.float32
    ).astype(jnp.bfloat16)
    return jnp.einsum("bfp,bsp->bfs", colloc, spread_back, preferred_element_type=jnp.float32)


def on_device(
    occ_coeffs,
    colloc,
    grid_points,
    grid_weights,
    charge_sites,
    charge_proj,
    shell_lists,
    point_counts,
):
    row_count = lax.axis_size("row")
    col_count = lax.axis_size("col")
    owners = row_count * col_count
    me = lax.axis_index("row") * col_count + lax.axis_index("col")
    group_rows = occ_coeffs.shape[0]
    slab_width = charge_proj.shape[1]
    own_rows = group_rows // col_count
    own_blocks = own_rows // SH
    tile = SH * slab_width
    all_lists = lax.all_gather(shell_lists, ("row", "col"), tiled=True)
    window = broadcast_from_first(occ_coeffs[:slab_width], "row")
    requested = shell_lists.reshape(-1)
    request_count = requested.shape[0]
    capacity = 2 * request_count // owners
    slots = owners * capacity
    owner = requested // own_blocks
    onehot = (owner[:, None] == jnp.arange(owners)[None, :]).astype(jnp.int32)
    before = jnp.cumsum(onehot, axis=0) - onehot
    rank = jnp.sum(before * onehot, axis=1)
    slot = owner * capacity + rank
    pick = (slot[:, None] == jnp.arange(slots)[None, :]).astype(jnp.bfloat16)
    lists = all_lists.reshape(owners, request_count)
    mine = (lists // own_blocks == me).astype(jnp.int32)
    order = jnp.cumsum(mine, axis=1)
    local = lists % own_blocks
    wanted_by = []
    for place in range(capacity):
        hit = mine * (order == place + 1)
        wanted_by.append(jnp.sum(hit * (local + 1), axis=1) - 1)
    received_ids = jnp.stack(wanted_by, axis=1).reshape(-1)
    serve = (received_ids[:, None] == jnp.arange(own_blocks)[None, :]).astype(jnp.bfloat16)
    density = lax.psum_scatter(
        lax.dot_general(
            occ_coeffs, window, (((1,), (1,)), ((), ())), preferred_element_type=jnp.float32
        ),
        "col",
        scatter_dimension=0,
        tiled=True,
    ).astype(jnp.bfloat16)
    store = density.reshape(own_blocks, tile)
    found = jnp.dot(serve, store, preferred_element_type=jnp.float32).astype(jnp.bfloat16)
    replies = lax.all_to_all(
        found.reshape(owners, capacity, tile),
        ("row", "col"),
        split_axis=0,
        concat_axis=0,
        tiled=True,
    )
    fetched = jnp.dot(
        pick, replies.reshape(slots, tile), preferred_element_type=jnp.float32
    ).astype(jnp.bfloat16)
    dens_rows = fetched.reshape(shell_lists.shape[0], NSIG * SH, slab_width)
    terms = batch_terms(
        dens_rows, colloc, grid_points, grid_weights, charge_sites, charge_proj, point_counts
    )
    terms = terms.astype(jnp.bfloat16).reshape(request_count, tile)
    tiles = lax.dot_general(
        pick, terms, (((0,), (0,)), ((), ())), preferred_element_type=jnp.float32
    ).astype(jnp.bfloat16)
    arrived = lax.all_to_all(
        tiles.reshape(owners, capacity, tile),
        ("row", "col"),
        split_axis=0,
        concat_axis=0,
        tiled=True,
    )
    summed = lax.dot_general(
        serve,
        arrived.reshape(slots, tile),
        (((0,), (0,)), ((), ())),
        preferred_element_type=jnp.float32,
    )
    return summed.reshape(own_rows, slab_width)


def solution(mesh):
    placed = (
        P("row", "col"),
        P(("row", "col"), None, None),
        P(("row", "col"), None, None),
        P(("row", "col"), None),
        P(),
        P(),
        P(("row", "col"), None),
        P(("row", "col")),
    )
    return jax.shard_map(
        on_device, mesh=mesh, in_specs=placed, out_specs=P(("row", "col"), None), check_vma=False
    )
```

profile of v0, /device:TPU:1, one launch (start us, length us, event | category | flops | bytes accessed | tf_op | source)
XLA Modules:
  0.0 319.2 jit_solution(13722545505886730577)
XLA Ops:
  6.5 1.0 slice.21
  7.6 1.3 collective-permute-start
  8.9 2.5 collective-permute-done
  11.4 1.0 broadcast_select_fusion
  12.4 1.3 collective-permute-start.1
  13.7 6.8 %collective-permute-done.1 = bf16[128,1280]{1,0:T(8,128)(2,1)S(1)} collective-permute-done((bf16[128,1280]{1,0:T(8,128)(2,1)S(1)}, bf16[128,1280]{1,0:T(8,128)(2,1)S(1)}, u32[]{:S(2)}, u32[]{:S(2)}) %collective-permute-start.1) | collective-permute-done | bytes 327712 | tf_op jit(solution)/shard_map/ppermute | solution.py:17
  20.5 1.3 collective-permute-start.2
  21.9 6.1 %collective-permute-done.2 = bf16[128,1280]{1,0:T(8,128)(2,1)S(1)} collective-permute-done((bf16[128,1280]{1,0:T(8,128)(2,1)S(1)}, bf16[128,1280]{1,0:T(8,128)(2,1)S(1)}, u32[]{:S(2)}, u32[]{:S(2)}) %collective-permute-start.2) | collective-permute-done | bytes 327712 | tf_op jit(solution)/shard_map/ppermute | solution.py:17
  28.0 12.3 %convolution_bitcast_fusion = f32[6144,128]{0,1:T(8,128)} fusion(bf16[6144,1280]{1,0:T(8,128)(2,1)} %param.8, bf16[128,1280]{1,0:T(8,128)(2,1)S(1)} %collective-permute-done.2, bf16[128,1280]{1,0:T(8,128)(2,1)S(1)} %broadcast_select_fusion.1, pred[]{:T(512)S(6)} %ge.9), kind=kOutput, calls=%fused_computation.6 | convolution fusion | flops 2013429760 | bytes 19529728 | tf_op jit(solution)/shard_map/dot_general | solution.py:90
  40.3 61.2 %all_gather.3 = s32[1024,16]{1,0:T(8,128)S(1)} all-gather(s32[8,16]{1,0:T(8,128)S(1)} %copy-done.3), channel_id=1, replica_groups=mesh['row'=8,'col'=16] {'row','col'}, dimensions={0}, use_global_device_ids=true | all-gather | bytes 66048 | tf_op jit(solution)/shard_map/all_gather | solution.py:67
  101.5 0.1 broadcast_divide_fusion
  101.7 0.2 div.28
  101.9 0.3 fusion.15
  102.2 0.2 and.32
  102.6 0.2 reduce_window_sum.22
  102.8 0.1 copy.13
  102.9 0.2 eq.75
  103.1 0.1 copy.14
  103.3 0.2 eq.80
  103.5 0.9 fusion.10
  104.5 0.1 reduce_sum.36
  104.7 0.1 reduce_sum.46
  104.8 0.1 copy.15
  104.9 0.1 eq.81
  105.1 17.2 %reduce-scatter.2.cloned.1.call-done = f32[384,128]{0,1:T(8,128)} async-done(((f32[6144,128]{0,1:T(8,128)}), f32[384,128]{0,1:T(8,128)}) %reduce-scatter.2.cloned.1.call-update) | async-done | bytes 196624 | tf_op jit(solution)/shard_map/reduce_scatter | solution.py:89
  122.2 0.9 convert_element_type.46
  123.2 0.1 copy.16
  123.3 0.1 reshape.107
  123.4 3.2 %convolution_convert_fusion.1 = bf16[256,8192]{1,0:T(8,128)(2,1)} fusion(bf16[6,8192]{1,0:T(8,128)(2,1)S(1)} %reshape.107, s32[256]{0:T(256)S(1)} %eq.81), kind=kOutput, calls=%fused_computation.1 | convolution fusion | flops 27264512 | bytes 4293632 | tf_op jit(solution)/shard_map/dot_general | solution.py:98
  126.7 7.6 %reshape.108 = bf16[128,2,8192]{2,1,0:T(2,128)(2,1)} reshape(bf16[256,8192]{1,0:T(8,128)(2,1)} %convolution_convert_fusion.1) | data formatting | bytes 8388608 | tf_op jit(solution)/shard_map/reshape | solution.py:100
  134.3 9.6 %all-to-all-start = ((bf16[128,2,8192]{2,1,0:T(2,128)(2,1)}), bf16[128,2,8192]{2,1,0:T(2,128)(2,1)}, u32[]{:S(2)}, u32[]{:S(2)}) async-start(bf16[128,2,8192]{2,1,0:T(2,128)(2,1)} %reshape.108), calls=%async_computation.1 | async-start | bytes 8388608 | tf_op jit(solution)/shard_map/all_to_all | solution.py:99
  144.2 0.2 reduce_window_sum.23
  144.4 0.2 select_reduce_fusion
  144.7 51.3 %all-to-all-done = bf16[128,2,8192]{2,1,0:T(2,128)(2,1)} async-done(((bf16[128,2,8192]{2,1,0:T(2,128)(2,1)}), bf16[128,2,8192]{2,1,0:T(2,128)(2,1)}, u32[]{:S(2)}, u32[]{:S(2)}) %all-to-all-start) | async-done | bytes 4194336 | tf_op jit(solution)/shard_map/all_to_all | solution.py:99
  196.0 7.2 %reshape.109 = bf16[256,8192]{1,0:T(8,128)(2,1)} reshape(bf16[128,2,8192]{2,1,0:T(2,128)(2,1)} %all-to-all-done) | data formatting | bytes 8388608 | tf_op jit(solution)/shard_map/reshape | solution.py:107
  203.2 4.3 %convolution_convert_fusion.2 = bf16[128,8192]{1,0:T(8,128)(2,1)} fusion(bf16[256,8192]{1,0:T(8,128)(2,1)} %reshape.109, s32[128]{0:T(128)S(1)} %multiply_add_fusion), kind=kOutput, calls=%fused_computation.2 | convolution fusion | flops 537952256 | bytes 6291968 | tf_op jit(solution)/shard_map/dot_general | solution.py:106
  207.5 2.9 reshape.110
  210.4 4.8 %convolution_convert_fusion.3 = bf16[8,128,512]{2,1,0:T(8,128)(2,1)S(1)} fusion(bf16[8,1024,128]{2,1,0:T(8,128)(2,1)S(1)} %reshape.110, bf16[8,1024,512]{2,1,0:T(8,128)(2,1)} %param.9), kind=kOutput, calls=%fused_computation.11 | convolution fusion | flops 1074266112 | bytes 11534336 | tf_op jit(solution)/shard_map/bfs,bfp->bsp/dot_general | solution.py:34
  215.2 5.9 %fusion.6 = bf16[8,512,128]{1,2,0:T(8,128)(2,1)} fusion(f32[8,512]{1,0:T(8,128)S(1)} %fusion.28, f32[512]{0:T(512)S(1)} %bitcast.41, f32[8,512]{1,0:T(8,128)S(1)} %get-tuple-element.10, f32[512]{0:T(512)S(1)} %bitcast.42, f32[8,512]{1,0:T(8,128)S(1)} %get-tuple-element.11, f32[512]{0:T(512)S(1)} %bitcast.40, f32[8,512]{1,0:T(8,128)S(1)} %get-tuple-element.9, ...), kind=kOutput, calls=%fused_computation.10 | convolution fusion | flops 1099431936 | bytes 2299904 | tf_op jit(solution)/shard_map/ks,bkp->bsp/dot_general | solution.py:42
  221.1 6.5 %convert_bitcast_fusion = bf16[8,1024,128]{1,2,0:T(8,128)(2,1)S(1)} fusion(bf16[8,512,128]{1,2,0:T(8,128)(2,1)} %fusion.6, bf16[8,1024,512]{2,1,0:T(8,128)(2,1)} %param.9), kind=kOutput, calls=%fused_computation.9 | convolution fusion | flops 1074790400 | bytes 11534336 | tf_op jit(solution)/shard_map/bfp,bsp->bfs/dot_general | solution.py:45
  227.6 2.4 copy.17
  230.0 2.8 reshape.111
  232.8 3.3 %convolution_convert_fusion = bf16[256,8192]{1,0:T(8,128)(2,1)} fusion(bf16[128,8192]{1,0:T(8,128)(2,1)S(1)} %reshape.111, s32[128]{0:T(128)S(1)} %multiply_add_fusion), kind=kOutput, calls=%fused_computation | convolution fusion | flops 539000832 | bytes 6291968 | tf_op jit(solution)/shard_map/dot_general | solution.py:114
  236.2 7.6 %reshape.112 = bf16[128,2,8192]{2,1,0:T(2,128)(2,1)} reshape(bf16[256,8192]{1,0:T(8,128)(2,1)} %convolution_convert_fusion) | data formatting | bytes 8388608 | tf_op jit(solution)/shard_map/reshape | solution.py:118
  243.8 57.6 %all_to_all.10 = bf16[128,2,8192]{2,1,0:T(2,128)(2,1)} all-to-all(bf16[128,2,8192]{2,1,0:T(2,128)(2,1)} %reshape.112), channel_id=1, replica_groups=mesh['row'=8,'col'=16] {'row','col'}, dimensions={0} | all-to-all | bytes 8388608 | tf_op jit(solution)/shard_map/all_to_all | solution.py:117
  301.4 7.2 %reshape.113 = bf16[256,8192]{1,0:T(8,128)(2,1)} reshape(bf16[128,2,8192]{2,1,0:T(2,128)(2,1)} %all_to_all.10) | data formatting | bytes 8388608 | tf_op jit(solution)/shard_map/reshape | solution.py:126
  308.6 2.9 fusion.20
  311.5 0.8 reshape.114
  (34 shorter events, 0.8 us)
Async XLA Ops:
  6.5 208.6 %copy-start = (bf16[512,128]{1,0:T(8,128)(2,1)S(1)}, bf16[512,128]{1,0:T(8,128)(2,1)}, u32[]{:S(2)}) copy-start(bf16[512,128]{1,0:T(8,128)(2,1)} %param.13) | copy-start | bytes 393220
  6.5 115.7 %reduce-scatter.2.cloned.1.call-start = ((), (), s32[]{:S(2)}) async-start(), calls=%async_computation.3 | async-start | bytes 3342336 | tf_op jit(solution)/shard_map/reduce_scatter | solution.py:89
  7.6 3.8 %collective-permute-start = (bf16[128,1280]{1,0:T(8,128)(2,1)S(1)}, bf16[128,1280]{1,0:T(8,128)(2,1)S(1)}, u32[]{:S(2)}, u32[]{:S(2)}) collective-permute-start(bf16[128,1280]{1,0:T(8,128)(2,1)S(1)} %slice.21), channel_id=1, source_target_pairs={{0,16},{1,17},{2,18},{3,19},{4,20},{5,21},{6,22},{7,23},{8,24},{9,... | collective-permute-start | bytes 983048 | tf_op jit(solution)/shard_map/ppermute | solution.py:17
  12.4 8.1 %collective-permute-start.1 = (bf16[128,1280]{1,0:T(8,128)(2,1)S(1)}, bf16[128,1280]{1,0:T(8,128)(2,1)S(1)}, u32[]{:S(2)}, u32[]{:S(2)}) collective-permute-start(bf16[128,1280]{1,0:T(8,128)(2,1)S(1)} %broadcast_select_fusion), channel_id=1, source_target_pairs={{0,32},{16,48},{1,33},{17,49},{2,34},{18,50},{3,35},{19,51},{4,36}... | collective-permute-start | bytes 983048 | tf_op jit(solution)/shard_map/ppermute | solution.py:17
  20.5 7.5 %collective-permute-start.2 = (bf16[128,1280]{1,0:T(8,128)(2,1)S(1)}, bf16[128,1280]{1,0:T(8,128)(2,1)S(1)}, u32[]{:S(2)}, u32[]{:S(2)}) collective-permute-start(bf16[128,1280]{1,0:T(8,128)(2,1)S(1)} %broadcast_select_fusion.1), channel_id=1, source_target_pairs={{0,64},{16,80},{32,96},{48,112},{1,65},{17,81},{33,97},{49,113},{2... | collective-permute-start | bytes 983048 | tf_op jit(solution)/shard_map/ppermute | solution.py:17
  21.8 18.5 %copy-start.3 = (s32[8,16]{1,0:T(8,128)S(1)}, s32[8,16]{1,0:T(8,128)}, u32[]{:S(2)}) copy-start(s32[8,16]{1,0:T(8,128)} %param.14) | copy-start | bytes 1540
  134.3 10.3 %copy-start.5 = (f32[3,512]{1,0:T(4,128)S(1)}, f32[3,512]{1,0:T(4,128)}, u32[]{:S(2)}) copy-start(f32[3,512]{1,0:T(4,128)} %param.12) | copy-start | bytes 18436
  134.3 10.3 %copy-start.4 = (f32[8,512]{1,0:T(8,128)S(1)}, f32[8,512]{1,0:T(8,128)}, u32[]{:S(2)}) copy-start(f32[8,512]{1,0:T(8,128)} %param.11) | copy-start | bytes 49156
  134.3 10.3 %copy-start.6 = (s32[8]{0:T(128)S(1)}, s32[8]{0:T(128)}, u32[]{:S(2)}) copy-start(s32[8]{0:T(128)} %param.15) | copy-start | bytes 100
  134.3 10.4 %copy-start.2 = (f32[8,3,512]{2,0,1:T(8,128)S(1)}, f32[8,3,512]{2,0,1:T(8,128)}, u32[]{:S(2)}) copy-start(f32[8,3,512]{2,0,1:T(8,128)} %param.10) | copy-start | bytes 147460
  134.3 61.7 %all-to-all-start = ((bf16[128,2,8192]{2,1,0:T(2,128)(2,1)}), bf16[128,2,8192]{2,1,0:T(2,128)(2,1)}, u32[]{:S(2)}, u32[]{:S(2)}) async-start(bf16[128,2,8192]{2,1,0:T(2,128)(2,1)} %reshape.108), calls=%async_computation.1 | async-start | bytes 8388608 | tf_op jit(solution)/shard_map/all_to_all | solution.py:99
  301.4 11.0 %copy-start.1 = (bf16[512,128]{1,0:T(8,128)(2,1)S(1)}, bf16[512,128]{1,0:T(8,128)(2,1)}, u32[]{:S(2)}) copy-start(bf16[512,128]{1,0:T(8,128)(2,1)} %param.13) | copy-start | bytes 393220
Sparse Core Ops, SparseCore 0:
  40.4 81.7 reduce-scatter.1
where the time goes:
time: 321 us; the launch traced here: 319 us
  blocking collectives  119 us (37%)
  waiting for transfers between devices  83.9 us (26%)
  matrix products  43.3 us (13%)
  local copies, waits for them, and re-layouts  41.7 us (13%)
  between operations  13.7 us (4%)
  starting transfers between devices  13.5 us (4%)
  other arithmetic  4.28 us (1%)
    all_gather x1, blocking collectives, on_device(): all_lists = lax.all_gather(shell_lists, ('row', 'col'), tiled=True)  61.2 us
    all_to_all x1, blocking collectives, on_device(): lax.all_to_all(tiles.reshape(owners, capacity, tile), ('row', 'col'), spl...  57.6 us
    all_to_all x1, waiting for transfers between devices, on_device(): lax.all_to_all(found.reshape(owners, capacity, tile), ('row', 'col'), spl...  51.3 us
    reduce_scatter x1, waiting for transfers between devices, on_device(): lax.psum_scatter(lax.dot_general(occ_coeffs, window, (((1,), (1,)), ((),...  17.2 us
    ppermute x3, waiting for transfers between devices, broadcast_from_first(): moved = lax.ppermute(value, axis, pairs)  15.4 us
    dot_general x1, matrix products, on_device(): lax.dot_general(occ_coeffs, window, (((1,), (1,)), ((), ())), preferred_e...  12.3 us
    all_to_all x1, starting transfers between devices, on_device(): lax.all_to_all(found.reshape(owners, capacity, tile), ('row', 'col'), spl...  9.57 us
    reshape x1, local copies, waits for them, and re-layouts, on_device(): found.reshape(owners, capacity, tile)  7.62 us
  transfers between devices with their start and end apart: 5, of which 5 were waited for; matrix products, arithmetic and copies ran while one was open for 1% of the time, Pallas kernels for 0%

commit v1 on v0

--- a/solution.py
+++ b/solution.py
@@ -64,7 +64,12 @@
     own_rows = group_rows // col_count
     own_blocks = own_rows // SH
     tile = SH * slab_width
-    all_lists = lax.all_gather(shell_lists, ("row", "col"), tiled=True)
+    all_lists = jnp.concatenate(
+        lax.all_to_all(
+            jnp.stack([shell_lists] * lax.axis_size(("row", "col"))), ("row", "col"), 0, 0
+        ),
+        axis=0,
+    )
     window = broadcast_from_first(occ_coeffs[:slab_width], "row")
     requested = shell_lists.reshape(-1)
     request_count = requested.shape[0]

time: 321 us -> 320 us (level)
  blocking collectives: 119 us -> 57.6 us
  waiting for transfers between devices: 83.9 us -> 129 us
  starting transfers between devices: 13.5 us -> 28.6 us
    all_gather x1 -> x0, blocking collectives: 61.2 us -> none  [on_device(): all_lists = lax.all_gather(shell_lists, ('row', 'col'), tiled=True)]
    reduce_scatter x1, waiting for transfers between devices: 17.2 us -> 53.3 us  [on_device(): lax.psum_scatter(lax.dot_general(occ_coeffs, window, (((1,), (1,)), ((),...]
    all_to_all x0 -> x1, starting transfers between devices: none -> 15.1 us  [on_device(): lax.all_to_all(jnp.stack([shell_lists] * lax.axis_size(('row', 'col'))),...]
    all_to_all x0 -> x1, waiting for transfers between devices: none -> 9.47 us  [on_device(): lax.all_to_all(jnp.stack([shell_lists] * lax.axis_size(('row', 'col'))),...]
  transfers between devices with their start and end apart: 5 -> 6, of which waited for: 5 -> 6; matrix products, arithmetic and copies ran while one was open for 1% -> 1% of each run, Pallas kernels for 0% -> 0%
where the time goes in v1:
time: 320 us; the launch traced here: 318 us
  waiting for transfers between devices  129 us (40%)
  blocking collectives  57.6 us (18%)
  matrix products  43.2 us (14%)
  local copies, waits for them, and re-layouts  42.1 us (13%)
  starting transfers between devices  28.6 us (9%)
  between operations  13.7 us (4%)
  other arithmetic  3.73 us (1%)
    all_to_all x1, blocking collectives, on_device(): lax.all_to_all(tiles.reshape(owners, capacity, tile), ('row', 'col'), spl...  57.6 us
    reduce_scatter x1, waiting for transfers between devices, on_device(): lax.psum_scatter(lax.dot_general(occ_coeffs, window, (((1,), (1,)), ((),...  53.3 us
    all_to_all x1, waiting for transfers between devices, on_device(): lax.all_to_all(found.reshape(owners, capacity, tile), ('row', 'col'), spl...  51.3 us
    ppermute x3, waiting for transfers between devices, broadcast_from_first(): moved = lax.ppermute(value, axis, pairs)  15.4 us
    all_to_all x1, starting transfers between devices, on_device(): lax.all_to_all(jnp.stack([shell_lists] * lax.axis_size(('row', 'col'))),...  15.1 us
    dot_general x1, matrix products, on_device(): lax.dot_general(occ_coeffs, window, (((1,), (1,)), ((), ())), preferred_e...  12.3 us
    all_to_all x1, starting transfers between devices, on_device(): lax.all_to_all(found.reshape(owners, capacity, tile), ('row', 'col'), spl...  9.59 us
    all_to_all x1, waiting for transfers between devices, on_device(): lax.all_to_all(jnp.stack([shell_lists] * lax.axis_size(('row', 'col'))),...  9.47 us
  transfers between devices with their start and end apart: 6, of which 6 were waited for; matrix products, arithmetic and copies ran while one was open for 1% of the time, Pallas kernels for 0%

profile of v1, /device:TPU:1, one launch (start us, length us, event | category | flops | bytes accessed | tf_op | source)
XLA Modules:
  0.0 318.3 jit_solution(11947451546033048476)
XLA Ops:
  6.5 1.0 slice.21
  7.6 1.3 collective-permute-start
  8.9 2.5 collective-permute-done
  11.4 1.0 broadcast_select_fusion
  12.4 1.3 collective-permute-start.1
  13.7 6.8 %collective-permute-done.1 = bf16[128,1280]{1,0:T(8,128)(2,1)S(1)} collective-permute-done((bf16[128,1280]{1,0:T(8,128)(2,1)S(1)}, bf16[128,1280]{1,0:T(8,128)(2,1)S(1)}, u32[]{:S(2)}, u32[]{:S(2)}) %collective-permute-start.1) | collective-permute-done | bytes 327712 | tf_op jit(solution)/shard_map/ppermute | solution.py:17
  20.5 1.3 collective-permute-start.2
  21.9 6.1 %collective-permute-done.2 = bf16[128,1280]{1,0:T(8,128)(2,1)S(1)} collective-permute-done((bf16[128,1280]{1,0:T(8,128)(2,1)S(1)}, bf16[128,1280]{1,0:T(8,128)(2,1)S(1)}, u32[]{:S(2)}, u32[]{:S(2)}) %collective-permute-start.2) | collective-permute-done | bytes 327712 | tf_op jit(solution)/shard_map/ppermute | solution.py:17
  28.0 12.3 %convolution_bitcast_fusion = f32[6144,128]{0,1:T(8,128)} fusion(bf16[6144,1280]{1,0:T(8,128)(2,1)} %param.8, bf16[128,1280]{1,0:T(8,128)(2,1)S(1)} %collective-permute-done.2, bf16[128,1280]{1,0:T(8,128)(2,1)S(1)} %broadcast_select_fusion.1, pred[]{:T(512)S(6)} %ge.9), kind=kOutput, calls=%fused_computation.6 | convolution fusion | flops 2013429760 | bytes 19529728 | tf_op jit(solution)/shard_map/dot_general | solution.py:95
  40.3 0.9 reshape.115
  41.2 15.1 %all-to-all-start = ((s32[128,1,128]{2,1,0:T(1,128)}), s32[128,1,128]{2,1,0:T(1,128)S(1)}, u32[]{:S(2)}, u32[]{:S(2)}) async-start(s32[128,1,128]{2,1,0:T(1,128)} %reshape.115), calls=%async_computation | async-start | bytes 131072 | tf_op jit(solution)/shard_map/all_to_all | solution.py:68
  56.3 9.5 %all-to-all-done = s32[128,1,128]{2,1,0:T(1,128)S(1)} async-done(((s32[128,1,128]{2,1,0:T(1,128)}), s32[128,1,128]{2,1,0:T(1,128)S(1)}, u32[]{:S(2)}, u32[]{:S(2)}) %all-to-all-start) | async-done | bytes 65568 | tf_op jit(solution)/shard_map/all_to_all | solution.py:68
  65.8 0.5 broadcast.138
  66.3 0.8 reduce.2
  67.1 0.2 reshape.116
  67.3 0.2 copy.23
  67.6 0.2 reduce_window_sum.22
  67.8 0.1 fusion.15
  67.9 0.1 copy.26
  68.0 0.1 eq.81
  68.2 53.3 %reduce-scatter.2.cloned.1.call-done = f32[384,128]{0,1:T(8,128)} async-done(((f32[6144,128]{0,1:T(8,128)}), f32[384,128]{0,1:T(8,128)}) %reduce-scatter.2.cloned.1.call-update) | async-done | bytes 196624 | tf_op jit(solution)/shard_map/reduce_scatter | solution.py:94
  121.5 0.9 convert_element_type.46
  122.4 0.1 copy.27
  122.6 0.1 reshape.106
  122.7 3.2 %convolution_convert_fusion.1 = bf16[256,8192]{1,0:T(8,128)(2,1)} fusion(bf16[6,8192]{1,0:T(8,128)(2,1)S(1)} %reshape.106, s32[256]{0:T(256)S(1)} %eq.81), kind=kOutput, calls=%fused_computation.1 | convolution fusion | flops 27264512 | bytes 4293632 | tf_op jit(solution)/shard_map/dot_general | solution.py:103
  125.9 7.6 %reshape.107 = bf16[128,2,8192]{2,1,0:T(2,128)(2,1)} reshape(bf16[256,8192]{1,0:T(8,128)(2,1)} %convolution_convert_fusion.1) | data formatting | bytes 8388608 | tf_op jit(solution)/shard_map/reshape | solution.py:105
  133.6 9.6 %all-to-all-start.1 = ((bf16[128,2,8192]{2,1,0:T(2,128)(2,1)}), bf16[128,2,8192]{2,1,0:T(2,128)(2,1)}, u32[]{:S(2)}, u32[]{:S(2)}) async-start(bf16[128,2,8192]{2,1,0:T(2,128)(2,1)} %reshape.107), calls=%async_computation.2 | async-start | bytes 8388608 | tf_op jit(solution)/shard_map/all_to_all | solution.py:104
  143.2 0.1 div.30
  143.3 0.1 and.35
  143.4 0.1 fusion.23
  143.5 0.2 reduce_window_sum.23
  143.6 0.2 select_reduce_fusion
  143.9 0.1 fusion.28
  144.0 51.3 %all-to-all-done.1 = bf16[128,2,8192]{2,1,0:T(2,128)(2,1)} async-done(((bf16[128,2,8192]{2,1,0:T(2,128)(2,1)}), bf16[128,2,8192]{2,1,0:T(2,128)(2,1)}, u32[]{:S(2)}, u32[]{:S(2)}) %all-to-all-start.1) | async-done | bytes 4194336 | tf_op jit(solution)/shard_map/all_to_all | solution.py:104
  195.3 7.2 %reshape.108 = bf16[256,8192]{1,0:T(8,128)(2,1)} reshape(bf16[128,2,8192]{2,1,0:T(2,128)(2,1)} %all-to-all-done.1) | data formatting | bytes 8388608 | tf_op jit(solution)/shard_map/reshape | solution.py:112
  202.5 4.3 %convolution_convert_fusion.2 = bf16[128,8192]{1,0:T(8,128)(2,1)} fusion(bf16[256,8192]{1,0:T(8,128)(2,1)} %reshape.108, s32[128]{0:T(128)S(1)} %multiply_add_fusion), kind=kOutput, calls=%fused_computation.2 | convolution fusion | flops 537952256 | bytes 6291968 | tf_op jit(solution)/shard_map/dot_general | solution.py:111
  206.8 2.9 reshape.109
  209.6 4.8 %convolution_convert_fusion.3 = bf16[8,128,512]{2,1,0:T(8,128)(2,1)S(1)} fusion(bf16[8,1024,128]{2,1,0:T(8,128)(2,1)S(1)} %reshape.109, bf16[8,1024,512]{2,1,0:T(8,128)(2,1)} %param.9), kind=kOutput, calls=%fused_computation.11 | convolution fusion | flops 1074266112 | bytes 11534336 | tf_op jit(solution)/shard_map/bfs,bfp->bsp/dot_general | solution.py:34
  214.4 5.7 %fusion.6 = bf16[8,512,128]{2,1,0:T(8,128)(2,1)} fusion(f32[8,512]{1,0:T(8,128)S(1)} %fusion.28, f32[512]{0:T(512)S(1)} %bitcast.51, f32[8,512]{1,0:T(8,128)S(1)} %get-tuple-element.8, f32[512]{0:T(512)S(1)} %bitcast.52, f32[8,512]{1,0:T(8,128)S(1)} %get-tuple-element.9, f32[512]{0:T(512)S(1)} %bitcast.50, f32[8,512]{1,0:T(8,128)S(1)} %get-tuple-element.7, ...), kind=kOutput, calls=%fused_computation.10 | convolution fusion | flops 1099431936 | bytes 2299904 | tf_op jit(solution)/shard_map/ks,bkp->bsp/dot_general | solution.py:42
  220.2 6.6 %convert_bitcast_fusion = bf16[8,1024,128]{1,2,0:T(8,128)(2,1)S(1)} fusion(bf16[8,512,128]{2,1,0:T(8,128)(2,1)} %fusion.6, bf16[8,1024,512]{2,1,0:T(8,128)(2,1)} %param.9), kind=kOutput, calls=%fused_computation.9 | convolution fusion | flops 1074790400 | bytes 11534336 | tf_op jit(solution)/shard_map/bfp,bsp->bfs/dot_general | solution.py:45
  226.8 2.4 copy.31
  229.2 2.8 reshape.110
  232.0 3.3 %convolution_convert_fusion = bf16[256,8192]{1,0:T(8,128)(2,1)} fusion(bf16[128,8192]{1,0:T(8,128)(2,1)S(1)} %reshape.110, s32[128]{0:T(128)S(1)} %multiply_add_fusion), kind=kOutput, calls=%fused_computation | convolution fusion | flops 539000832 | bytes 6291968 | tf_op jit(solution)/shard_map/dot_general | solution.py:119
  235.3 7.6 %reshape.111 = bf16[128,2,8192]{2,1,0:T(2,128)(2,1)} reshape(bf16[256,8192]{1,0:T(8,128)(2,1)} %convolution_convert_fusion) | data formatting | bytes 8388608 | tf_op jit(solution)/shard_map/reshape | solution.py:123
  242.9 57.6 %all_to_all.15 = bf16[128,2,8192]{2,1,0:T(2,128)(2,1)} all-to-all(bf16[128,2,8192]{2,1,0:T(2,128)(2,1)} %reshape.111), channel_id=1, replica_groups=mesh['row'=8,'col'=16] {'row','col'}, dimensions={0} | all-to-all | bytes 8388608 | tf_op jit(solution)/shard_map/all_to_all | solution.py:122
  300.5 7.2 %reshape.112 = bf16[256,8192]{1,0:T(8,128)(2,1)} reshape(bf16[128,2,8192]{2,1,0:T(2,128)(2,1)} %all_to_all.15) | data formatting | bytes 8388608 | tf_op jit(solution)/shard_map/reshape | solution.py:131
  307.8 2.9 fusion.13
  310.7 0.8 reshape.113
  (29 shorter events, 0.3 us)
Async XLA Ops:
  6.5 207.9 %copy-start = (bf16[512,128]{1,0:T(8,128)(2,1)S(1)}, bf16[512,128]{1,0:T(8,128)(2,1)}, u32[]{:S(2)}) copy-start(bf16[512,128]{1,0:T(8,128)(2,1)} %param.13) | copy-start | bytes 393220
  6.5 115.0 %reduce-scatter.2.cloned.1.call-start = ((), (), s32[]{:S(2)}) async-start(), calls=%async_computation.4 | async-start | bytes 3342336 | tf_op jit(solution)/shard_map/reduce_scatter | solution.py:94
  7.6 3.8 %collective-permute-start = (bf16[128,1280]{1,0:T(8,128)(2,1)S(1)}, bf16[128,1280]{1,0:T(8,128)(2,1)S(1)}, u32[]{:S(2)}, u32[]{:S(2)}) collective-permute-start(bf16[128,1280]{1,0:T(8,128)(2,1)S(1)} %slice.21), channel_id=1, source_target_pairs={{0,16},{1,17},{2,18},{3,19},{4,20},{5,21},{6,22},{7,23},{8,24},{9,... | collective-permute-start | bytes 983048 | tf_op jit(solution)/shard_map/ppermute | solution.py:17
  12.4 8.1 %collective-permute-start.1 = (bf16[128,1280]{1,0:T(8,128)(2,1)S(1)}, bf16[128,1280]{1,0:T(8,128)(2,1)S(1)}, u32[]{:S(2)}, u32[]{:S(2)}) collective-permute-start(bf16[128,1280]{1,0:T(8,128)(2,1)S(1)} %broadcast_select_fusion), channel_id=1, source_target_pairs={{0,32},{16,48},{1,33},{17,49},{2,34},{18,50},{3,35},{19,51},{4,36}... | collective-permute-start | bytes 983048 | tf_op jit(solution)/shard_map/ppermute | solution.py:17
  20.5 7.5 %collective-permute-start.2 = (bf16[128,1280]{1,0:T(8,128)(2,1)S(1)}, bf16[128,1280]{1,0:T(8,128)(2,1)S(1)}, u32[]{:S(2)}, u32[]{:S(2)}) collective-permute-start(bf16[128,1280]{1,0:T(8,128)(2,1)S(1)} %broadcast_select_fusion.1), channel_id=1, source_target_pairs={{0,64},{16,80},{32,96},{48,112},{1,65},{17,81},{33,97},{49,113},{2... | collective-permute-start | bytes 983048 | tf_op jit(solution)/shard_map/ppermute | solution.py:17
  21.8 18.5 %copy-start.3 = (s32[8,16]{1,0:T(8,128)S(1)}, s32[8,16]{1,0:T(8,128)}, u32[]{:S(2)}) copy-start(s32[8,16]{1,0:T(8,128)} %param.14) | copy-start | bytes 1540
  41.2 24.6 %all-to-all-start = ((s32[128,1,128]{2,1,0:T(1,128)}), s32[128,1,128]{2,1,0:T(1,128)S(1)}, u32[]{:S(2)}, u32[]{:S(2)}) async-start(s32[128,1,128]{2,1,0:T(1,128)} %reshape.115), calls=%async_computation | async-start | bytes 131072 | tf_op jit(solution)/shard_map/all_to_all | solution.py:68
  133.6 10.3 %copy-start.5 = (f32[3,512]{1,0:T(4,128)S(1)}, f32[3,512]{1,0:T(4,128)}, u32[]{:S(2)}) copy-start(f32[3,512]{1,0:T(4,128)} %param.12) | copy-start | bytes 18436
  133.6 10.3 %copy-start.4 = (f32[8,512]{1,0:T(8,128)S(1)}, f32[8,512]{1,0:T(8,128)}, u32[]{:S(2)}) copy-start(f32[8,512]{1,0:T(8,128)} %param.11) | copy-start | bytes 49156
  133.6 10.3 %copy-start.6 = (s32[8]{0:T(128)S(1)}, s32[8]{0:T(128)}, u32[]{:S(2)}) copy-start(s32[8]{0:T(128)} %param.15) | copy-start | bytes 100
  133.6 10.4 %copy-start.2 = (f32[8,3,512]{2,0,1:T(8,128)S(1)}, f32[8,3,512]{2,0,1:T(8,128)}, u32[]{:S(2)}) copy-start(f32[8,3,512]{2,0,1:T(8,128)} %param.10) | copy-start | bytes 147460
  133.6 61.7 %all-to-all-start.1 = ((bf16[128,2,8192]{2,1,0:T(2,128)(2,1)}), bf16[128,2,8192]{2,1,0:T(2,128)(2,1)}, u32[]{:S(2)}, u32[]{:S(2)}) async-start(bf16[128,2,8192]{2,1,0:T(2,128)(2,1)} %reshape.107), calls=%async_computation.2 | async-start | bytes 8388608 | tf_op jit(solution)/shard_map/all_to_all | solution.py:104
  300.5 11.0 %copy-start.1 = (bf16[512,128]{1,0:T(8,128)(2,1)S(1)}, bf16[512,128]{1,0:T(8,128)(2,1)}, u32[]{:S(2)}) copy-start(bf16[512,128]{1,0:T(8,128)(2,1)} %param.13) | copy-start | bytes 393220
Sparse Core Ops, SparseCore 0:
  40.4 81.0 reduce-scatter.1
